TPU v7x, 32 devices: a whole 2x2x4 slice. The times are simulated.
32 devices in a mesh: seq: 8 (over y, x, core), head: 4 (over z).
Axes of the slice: x: 2, y: 2, z: 4, core: 2. Of those that a mesh axis runs over, the one named last changes fastest.
Arguments:
- hidden: bfloat16 [4096, 2048], P(('seq', 'head')), may hold values from -41 to 41
- w_qkv: bfloat16 [2048, 3072], replicated, may hold values from -0.125 to 0.125
- w_out: bfloat16 [2048, 2048], replicated, may hold values from -0.125 to 0.125
- seg_ids: int32 [4096], replicated, may hold values from 0 to 7, never falling along the last dimension, each value on 1 to 2048 neighbouring positions
- live: int32 [4096], replicated, may hold values 0 or 1
- page_table: int32 [256], replicated, may hold values from 0 to 255, as said below
Outputs:
- mixed: bfloat16 [4096, 2048], P(('seq', 'head'))
- kv_pool: bfloat16 [8, 256, 16, 128], P('head', 'seq')
Inputs may be any that keep to these rules, and one draw needn't show every extreme that they name: `page_table`: A permutation of the 256 pages; pool shard r along seq holds pages r * 32 to (r + 1) * 32 - 1, and the 32 logical pages of each seq group go exactly 4 to each pool shard.
All inputs are finite; a program needn't handle non-finite values.
Results may differ from a plain program's by a relative error of at most 0.0059.
The roundings to bfloat16 on the way count: a program that leaves them out, or rounds other values in their place, can miss the bound.
Values may be sent and summed in bfloat16 or wider, within the bound.
No kernel may reach another device: no remote copies, remote signals or barrier semaphores. Data moves between devices by JAX's collectives and lax.ppermute only.
A program may use at most 128 MiB of HBM per device.

v0:
```python
import math

import jax
import jax.numpy as jnp
from jax import lax
from jax.sharding import PartitionSpec as P

KVH = 8
HD = 64
PAGE = 16
QPK = 4


def shards(hidden, w_qkv, w_out, seg_ids, live, page_table):
    heads_n = lax.axis_size("head")
    head_at = lax.axis_index("head")
    seq_at = lax.axis_index("seq")
    groups_here = KVH // heads_n
    per_group = (QPK + 2) * HD
    columns = groups_here * per_group
    w_here = lax.dynamic_slice_in_dim(w_qkv, head_at * columns, columns, 1)
    grouped = jnp.dot(
        lax.all_gather(hidden, "head", axis=0, tiled=True),
        w_here,
        preferred_element_type=jnp.float32,
    ).astype(jnp.bfloat16)
    group_rows = grouped.shape[0]
    shaped = grouped.reshape(group_rows, groups_here, QPK + 2, HD)
    queries = shaped[:, :, :QPK]
    keyvals = shaped[:, :, QPK:].reshape(group_rows, groups_here, 2 * HD)
    first_row = seq_at * group_rows
    q_index = first_row + jnp.arange(group_rows, dtype=jnp.int32)
    q_seg = lax.dynamic_slice_in_dim(seg_ids, first_row, group_rows, 0)
    start_max = jnp.full((groups_here, QPK, group_rows), -1e30, jnp.float32)
    start_total = jnp.zeros((groups_here, QPK, group_rows), jnp.float32)
    start_acc = jnp.zeros((groups_here, QPK, group_rows, HD), jnp.float32)
    carry = (start_max, start_total, start_acc)
    piece = lax.all_gather(keyvals, "seq", axis=0, tiled=True)
    rows = piece.shape[0]
    block = math.gcd(rows, 1024)

    def advance(state, number):
        offset = number * block
        kv_block = lax.dynamic_slice_in_dim(piece, offset, block, 0)
        k_index = offset + jnp.arange(block, dtype=jnp.int32)
        k_seg = lax.dynamic_slice_in_dim(seg_ids, offset, block, 0)
        k_live = lax.dynamic_slice_in_dim(live, offset, block, 0)
        active = (offset <= q_index[-1]) & (k_seg[0] <= q_seg[-1]) & (k_seg[-1] >= q_seg[0])

        def compute(inner):
            run_max, run_total, run_acc = inner
            allowed = (k_seg[None, :] == q_seg[:, None]) & (k_index[None, :] <= q_index[:, None])
            allowed = allowed & ((k_live[None, :] == 1) | (k_index[None, :] == q_index[:, None]))
            scores = (
                jnp.einsum(
                    "qgcd,kgd->gcqk",
                    queries,
                    kv_block[:, :, :HD],
                    preferred_element_type=jnp.float32,
                )
                * 0.015625
            )
            masked = jnp.where(allowed[None, None], scores, -1e30)
            new_max = jnp.maximum(run_max, jnp.max(masked, axis=-1))
            weights = jnp.where(allowed[None, None], jnp.exp(masked - new_max[..., None]), 0.0)
            factor = jnp.exp(run_max - new_max)
            new_total = run_total * factor + jnp.sum(weights, axis=-1)
            update = jnp.einsum(
                "gcqk,kgd->gcqd",
                weights.astype(jnp.bfloat16),
                kv_block[:, :, HD:],
                preferred_element_type=jnp.float32,
            )
            return (new_max, new_total, run_acc * factor[..., None] + update)

        return (lax.cond(active, compute, lambda inner: inner, state), None)

    carry, _ = lax.scan(advance, carry, jnp.arange(rows // block, dtype=jnp.int32))
    final_max, final_total, final_acc = carry
    attended = (final_acc / final_total[..., None]).transpose(2, 0, 1, 3)
    attended = attended.reshape(group_rows, groups_here * QPK * HD).astype(jnp.bfloat16)
    own_tokens = lax.all_to_all(attended, "head", split_axis=0, concat_axis=1, tiled=True)
    mixed = jnp.dot(own_tokens, w_out, preferred_element_type=jnp.float32).astype(jnp.bfloat16)
    page_count = group_rows // PAGE
    pages = keyvals.reshape(page_count, PAGE, groups_here, 2 * HD)
    table_mine = lax.dynamic_slice_in_dim(page_table, seq_at * page_count, page_count, 0)
    order = jnp.argsort(table_mine // page_count, stable=True)
    received = lax.all_to_all(pages[order], "seq", split_axis=0, concat_axis=0, tiled=True)
    arriving = jnp.argsort((page_table // page_count != seq_at).astype(jnp.int32), stable=True)[
        :page_count
    ]
    slots = page_table[arriving] % page_count
    kv_pool = jnp.zeros_like(received).at[slots].set(received).transpose(2, 0, 1, 3)
    return (mixed, kv_pool)


def solution(mesh):
    placed = (P(("seq", "head"), None), P(), P(), P(), P(), P())
    return jax.shard_map(
        shards,
        mesh=mesh,
        in_specs=placed,
        out_specs=(P(("seq", "head"), None), P("head", "seq", None, None)),
        check_vma=False,
    )
```

profile of v0, /device:TPU:6, one launch (start us, length us, event | category | flops | bytes accessed | tf_op | source)
XLA Modules:
  0.0 190.4 jit_solution(10362855352461067151)
XLA Ops:
  7.9 48.5 %all-gather.3.cloned.1.call-done = bf16[512,2048]{1,0:T(8,128)(2,1)} async-done(((bf16[128,2048]{1,0:T(8,128)(2,1)}), bf16[512,2048]{1,0:T(8,128)(2,1)}) %all-gather.3.cloned.1.call-update) | async-done | bytes 2097168 | tf_op jit(solution)/shard_map/all_gather | solution.py:23
  56.4 4.4 %fusion.17 = bf16[768,512]{1,0:T(8,128)(2,1)S(1)} fusion(bf16[512,2048]{1,0:T(8,128)(2,1)} %all-gather.3.cloned.1.call-done, bf16[2048,3072]{1,0:T(8,128)(2,1)} %param.11, s32[]{:T(128)S(6)} %select_n.66), kind=kOutput, calls=%fused_computation.27 | convolution fusion | flops 1611005952 | bytes 6029316 | tf_op jit(solution)/shard_map/dot_general | solution.py:22
  62.3 1.6 sort.35
  66.3 1.3 gather_fusion.1
  67.6 4.2 %all-to-all-start.1 = ((bf16[32,16,2,128]{3,1,2,0:T(8,128)(2,1)}), bf16[32,16,2,128]{3,1,2,0:T(8,128)(2,1)S(1)}, u32[]{:S(2)}, u32[]{:S(2)}) async-start(bf16[32,16,2,128]{3,1,2,0:T(8,128)(2,1)} %gather_fusion.1), calls=%async_computation.1 | async-start | bytes 524288 | tf_op jit(solution)/shard_map/all_to_all | solution.py:88
  71.8 18.7 %all-gather.5.cloned.1.call-done = bf16[4096,2,128]{0,2,1:T(8,128)(2,1)} async-done(((bf16[512,2,128]{0,2,1:T(8,128)(2,1)}), bf16[4096,2,128]{0,2,1:T(8,128)(2,1)}) %all-gather.5.cloned.1.call-update) | async-done | bytes 2097168 | tf_op jit(solution)/shard_map/all_gather | solution.py:38
  90.6 71.4 %while.14 = (s32[]{:T(128)}, f32[2,4,512]{2,1,0:T(4,128)S(1)}, f32[2,4,512]{2,1,0:T(4,128)S(1)}, f32[2,4,512,64]{2,3,1,0:T(8,128)S(1)}, s32[4]{0:T(128)S(1)}, /*...) while((s32[]{:T(128)}, f32[2,4,512]{2,1,0:T(4,128)S(1)}, ...), condition=%wide.region_5.6_spmd, body=%wide.region_0.5_spmd.sunk | while | flops 1131948032 | bytes 55877072 | solution.py:78
  103.3 15.4 %conditional.2 = ((f32[2,4,512]{2,1,0:T(4,128)S(1)}, f32[2,4,512]{2,1,0:T(4,128)S(1)}, f32[2,4,512,64]{2,3,1,0:T(8,128)S(1)})) conditional(s32[]{:T(128)} %convert_element_type.48, (f32[2,4,512]{2,1,0:T(4,128)S(1)}, f32[2,4,512]{2,1,0:T(4,128)S(1)}, f32[2,4,512,64]{2,3,1,0:T(8,128)S(1)}) %tuple.48, (s32[1024]{0:T(1024)S(1)}, s32[512]{0:T(512)S(1)}, ...), branch_computations={%region_1.1_spmd, %region_2.4_spmd} | conditional | flops 1131948032 | bytes 55864376 | solution.py:76
  105.1 3.8 %fusion = (f32[2,4,512]{2,1,0:T(4,128)S(1)}, f32[2,1024,512,4]{2,1,3,0:T(8,128)S(1)}) fusion(pred[512,1024]{0,1:T(8,128)(4,1)S(1)} %or_and_fusion, bf16[512,2,4,64]{0,3,2,1:T(8,128)(2,1)S(1)} %get-tuple-element.140, bf16[4096,2,128]{0,2,1:T(8,128)(2,1)} %get-tuple-element.139, s32[]{:T(128)} %get-tuple-element.138), kind=kOutput, calls=%fused_computation.5 | convolution fusion | flops 549449728 | bytes 18104832 | tf_op jit(solution)/shard_map/while/body/eval_jaxpr/cond/branch_1_fun/qgcd,kgd->gcqk/dot_general | solution.py:55
  108.9 4.0 %fusion.2 = f32[2,4,512]{2,1,0:T(4,128)S(1)} fusion(f32[2,1024,512,4]{2,1,3,0:T(8,128)S(1)} %get-tuple-element.201, f32[2,4,512]{2,1,0:T(4,128)S(1)} %max.4, pred[512,1024]{0,1:T(8,128)(4,1)S(1)} %or_and_fusion), kind=kLoop, calls=%fused_computation.7 | loop fusion | flops 20967424 | bytes 17334272 | tf_op jit(solution)/shard_map/while/body/eval_jaxpr/cond/branch_1_fun/reduce_sum | solution.py:67
  112.9 5.7 %fusion.6 = f32[2,4,512,64]{2,3,1,0:T(8,128)S(1)} fusion(f32[2,1024,512,4]{2,1,3,0:T(8,128)S(1)} %get-tuple-element.201, f32[2,4,512]{2,1,0:T(4,128)S(1)} %max.4, pred[512,1024]{0,1:T(8,128)(4,1)S(1)} %or_and_fusion, f32[2,4,512,64]{2,3,1,0:T(8,128)S(1)} %get-tuple-element.142, f32[2,4,512]{2,1,0:T(4,128)S(1)} %bitcast.78, ...), kind=kOutput, calls=%fused_computation.11 | convolution fusion | flops 558366720 | bytes 19694084 | tf_op jit(solution)/shard_map/while/body/eval_jaxpr/cond/branch_1_fun/gcqk,kgd->gcqd/dot_general | solution.py:68
  125.0 15.4 %conditional.2 = ((f32[2,4,512]{2,1,0:T(4,128)S(1)}, f32[2,4,512]{2,1,0:T(4,128)S(1)}, f32[2,4,512,64]{2,3,1,0:T(8,128)S(1)})) conditional(s32[]{:T(128)} %convert_element_type.48, (f32[2,4,512]{2,1,0:T(4,128)S(1)}, f32[2,4,512]{2,1,0:T(4,128)S(1)}, f32[2,4,512,64]{2,3,1,0:T(8,128)S(1)}) %tuple.48, (s32[1024]{0:T(1024)S(1)}, s32[512]{0:T(512)S(1)}, ...), branch_computations={%region_1.1_spmd, %region_2.4_spmd} | conditional | flops 1131948032 | bytes 55864376 | solution.py:76
  126.8 3.8 %fusion = (f32[2,4,512]{2,1,0:T(4,128)S(1)}, f32[2,1024,512,4]{2,1,3,0:T(8,128)S(1)}) fusion(pred[512,1024]{0,1:T(8,128)(4,1)S(1)} %or_and_fusion, bf16[512,2,4,64]{0,3,2,1:T(8,128)(2,1)S(1)} %get-tuple-element.140, bf16[4096,2,128]{0,2,1:T(8,128)(2,1)} %get-tuple-element.139, s32[]{:T(128)} %get-tuple-element.138), kind=kOutput, calls=%fused_computation.5 | convolution fusion | flops 549449728 | bytes 18104832 | tf_op jit(solution)/shard_map/while/body/eval_jaxpr/cond/branch_1_fun/qgcd,kgd->gcqk/dot_general | solution.py:55
  130.6 4.0 %fusion.2 = f32[2,4,512]{2,1,0:T(4,128)S(1)} fusion(f32[2,1024,512,4]{2,1,3,0:T(8,128)S(1)} %get-tuple-element.201, f32[2,4,512]{2,1,0:T(4,128)S(1)} %max.4, pred[512,1024]{0,1:T(8,128)(4,1)S(1)} %or_and_fusion), kind=kLoop, calls=%fused_computation.7 | loop fusion | flops 20967424 | bytes 17334272 | tf_op jit(solution)/shard_map/while/body/eval_jaxpr/cond/branch_1_fun/reduce_sum | solution.py:67
  134.6 5.7 %fusion.6 = f32[2,4,512,64]{2,3,1,0:T(8,128)S(1)} fusion(f32[2,1024,512,4]{2,1,3,0:T(8,128)S(1)} %get-tuple-element.201, f32[2,4,512]{2,1,0:T(4,128)S(1)} %max.4, pred[512,1024]{0,1:T(8,128)(4,1)S(1)} %or_and_fusion, f32[2,4,512,64]{2,3,1,0:T(8,128)S(1)} %get-tuple-element.142, f32[2,4,512]{2,1,0:T(4,128)S(1)} %bitcast.78, ...), kind=kOutput, calls=%fused_computation.11 | convolution fusion | flops 558366720 | bytes 19694084 | tf_op jit(solution)/shard_map/while/body/eval_jaxpr/cond/branch_1_fun/gcqk,kgd->gcqd/dot_general | solution.py:68
  146.7 15.3 %conditional.2 = ((f32[2,4,512]{2,1,0:T(4,128)S(1)}, f32[2,4,512]{2,1,0:T(4,128)S(1)}, f32[2,4,512,64]{2,3,1,0:T(8,128)S(1)})) conditional(s32[]{:T(128)} %convert_element_type.48, (f32[2,4,512]{2,1,0:T(4,128)S(1)}, f32[2,4,512]{2,1,0:T(4,128)S(1)}, f32[2,4,512,64]{2,3,1,0:T(8,128)S(1)}) %tuple.48, (s32[1024]{0:T(1024)S(1)}, s32[512]{0:T(512)S(1)}, ...), branch_computations={%region_1.1_spmd, %region_2.4_spmd} | conditional | flops 1131948032 | bytes 55864376 | solution.py:76
  148.4 3.8 %fusion = (f32[2,4,512]{2,1,0:T(4,128)S(1)}, f32[2,1024,512,4]{2,1,3,0:T(8,128)S(1)}) fusion(pred[512,1024]{0,1:T(8,128)(4,1)S(1)} %or_and_fusion, bf16[512,2,4,64]{0,3,2,1:T(8,128)(2,1)S(1)} %get-tuple-element.140, bf16[4096,2,128]{0,2,1:T(8,128)(2,1)} %get-tuple-element.139, s32[]{:T(128)} %get-tuple-element.138), kind=kOutput, calls=%fused_computation.5 | convolution fusion | flops 549449728 | bytes 18104832 | tf_op jit(solution)/shard_map/while/body/eval_jaxpr/cond/branch_1_fun/qgcd,kgd->gcqk/dot_general | solution.py:55
  152.2 4.0 %fusion.2 = f32[2,4,512]{2,1,0:T(4,128)S(1)} fusion(f32[2,1024,512,4]{2,1,3,0:T(8,128)S(1)} %get-tuple-element.201, f32[2,4,512]{2,1,0:T(4,128)S(1)} %max.4, pred[512,1024]{0,1:T(8,128)(4,1)S(1)} %or_and_fusion), kind=kLoop, calls=%fused_computation.7 | loop fusion | flops 20967424 | bytes 17334272 | tf_op jit(solution)/shard_map/while/body/eval_jaxpr/cond/branch_1_fun/reduce_sum | solution.py:67
  156.3 5.7 %fusion.6 = f32[2,4,512,64]{2,3,1,0:T(8,128)S(1)} fusion(f32[2,1024,512,4]{2,1,3,0:T(8,128)S(1)} %get-tuple-element.201, f32[2,4,512]{2,1,0:T(4,128)S(1)} %max.4, pred[512,1024]{0,1:T(8,128)(4,1)S(1)} %or_and_fusion, f32[2,4,512,64]{2,3,1,0:T(8,128)S(1)} %get-tuple-element.142, f32[2,4,512]{2,1,0:T(4,128)S(1)} %bitcast.78, ...), kind=kOutput, calls=%fused_computation.11 | convolution fusion | flops 558366720 | bytes 19694084 | tf_op jit(solution)/shard_map/while/body/eval_jaxpr/cond/branch_1_fun/gcqk,kgd->gcqd/dot_general | solution.py:68
  163.2 4.6 %all-to-all-start = ((bf16[4,128,512]{1,2,0:T(8,128)(2,1)}), bf16[4,128,512]{1,2,0:T(8,128)(2,1)S(1)}, u32[]{:S(2)}, u32[]{:S(2)}) async-start(bf16[4,128,512]{1,2,0:T(8,128)(2,1)} %copy.20), calls=%async_computation | async-start | bytes 1048576 | tf_op jit(solution)/shard_map/all_to_all | solution.py:82
  167.8 3.2 %sort.34 = (s32[256]{0:T(256)}, s32[256]{0:T(256)S(1)}) sort(s32[256]{0:T(256)S(1)} %compare_convert_fusion, s32[256]{0:T(256)S(1)} %iota.19), dimensions={0}, to_apply=%region_6.7 | sort | flops 2048 | bytes 4096 | tf_op jit(solution)/shard_map/jit(argsort)/sort | solution.py:89
  171.8 1.5 scatter_fusion
  174.0 4.1 %all-to-all-done = bf16[4,128,512]{1,2,0:T(8,128)(2,1)S(1)} async-done(((bf16[4,128,512]{1,2,0:T(8,128)(2,1)}), bf16[4,128,512]{1,2,0:T(8,128)(2,1)S(1)}, u32[]{:S(2)}, u32[]{:S(2)}) %all-to-all-start) | async-done | bytes 524320 | tf_op jit(solution)/shard_map/all_to_all | solution.py:82
  178.1 5.5 %convolution_convert_fusion = bf16[128,2048]{1,0:T(8,128)(2,1)} fusion(bf16[128,2048]{0,1:T(8,128)(2,1)S(1)} %bitcast.69, bf16[2048,2048]{1,0:T(8,128)(2,1)} %param.12), kind=kOutput, calls=%fused_computation.26 | convolution fusion | flops 1074003968 | bytes 9437184 | tf_op jit(solution)/shard_map/dot_general | solution.py:83
  (72 shorter events, 22.7 us)
Async XLA Ops:
  7.2 49.2 %all-gather.3.cloned.1.call-start = ((), (), s32[]{:S(2)}) async-start(), calls=%async_computation.2 | async-start | bytes 2621440 | tf_op jit(solution)/shard_map/all_gather | solution.py:23
  7.9 82.6 %all-gather.5.cloned.1.call-start = ((), (), s32[]{:S(2)}) async-start(), calls=%async_computation.3 | async-start | bytes 2359296 | tf_op jit(solution)/shard_map/all_gather | solution.py:38
  67.6 95.6 %all-to-all-start.1 = ((bf16[32,16,2,128]{3,1,2,0:T(8,128)(2,1)}), bf16[32,16,2,128]{3,1,2,0:T(8,128)(2,1)S(1)}, u32[]{:S(2)}, u32[]{:S(2)}) async-start(bf16[32,16,2,128]{3,1,2,0:T(8,128)(2,1)} %gather_fusion.1), calls=%async_computation.1 | async-start | bytes 524288 | tf_op jit(solution)/shard_map/all_to_all | solution.py:88
  90.6 77.2 %copy-start = (s32[256]{0:T(256)S(1)}, s32[256]{0:T(256)}, u32[]{:S(2)}) copy-start(s32[256]{0:T(256)} %param.15) | copy-start | bytes 3076
  163.2 14.9 %all-to-all-start = ((bf16[4,128,512]{1,2,0:T(8,128)(2,1)}), bf16[4,128,512]{1,2,0:T(8,128)(2,1)S(1)}, u32[]{:S(2)}, u32[]{:S(2)}) async-start(bf16[4,128,512]{1,2,0:T(8,128)(2,1)} %copy.20), calls=%async_computation | async-start | bytes 1048576 | tf_op jit(solution)/shard_map/all_to_all | solution.py:82
Sparse Core Ops, SparseCore 0:
  9.5 46.8 all-gather.2
  61.7 28.7 all-gather.4
where the time goes:
time: 194 us; the launch traced here: 190 us
  waiting for transfers between devices  71.9 us (37%)
  matrix products  38.4 us (20%)
  other arithmetic  23.1 us (12%)
  local copies, waits for them, and re-layouts  18.6 us (10%)
  loops' own time  15.5 us (8%)
  between operations  14.2 us (7%)
  starting transfers between devices  8.87 us (5%)
    all_gather x1, waiting for transfers between devices, shards(): lax.all_gather(hidden, 'head', axis=0, tiled=True)  48.5 us
    all_gather x1, waiting for transfers between devices, shards(): piece = lax.all_gather(keyvals, 'seq', axis=0, tiled=True)  18.7 us
    dot_general x3, matrix products, compute(): jnp.einsum('gcqk,kgd->gcqd', weights.astype(jnp.bfloat16), kv_block[:, :,...  17.2 us
    another operation x1, loops' own time, shards(): lax.scan(advance, carry, jnp.arange(rows // block, dtype=jnp.int32))  15.3 us
    reduce_sum x3, other arithmetic, compute(): new_total = run_total * factor + jnp.sum(weights, axis=-1)  12.1 us
    dot_general x3, matrix products, compute(): jnp.einsum('qgcd,kgd->gcqk', queries, kv_block[:, :, :HD], preferred_elem...  11.3 us
    dot_general x1, matrix products, shards(): jnp.dot(own_tokens, w_out, preferred_element_type=jnp.float32)  5.46 us
    all_to_all x1, starting transfers between devices, shards(): lax.all_to_all(attended, 'head', split_axis=0, concat_axis=1, tiled=True)  4.6 us
  transfers between devices with their start and end apart: 4, of which 3 were waited for; matrix products, arithmetic and copies ran while one was open for 36% of the time, Pallas kernels for 0%

commit v1 on v0

--- a/solution.py
+++ b/solution.py
@@ -18,12 +18,10 @@
     groups_here = KVH // heads_n
     per_group = (QPK + 2) * HD
     columns = groups_here * per_group
-    w_here = lax.dynamic_slice_in_dim(w_qkv, head_at * columns, columns, 1)
-    grouped = jnp.dot(
-        lax.all_gather(hidden, "head", axis=0, tiled=True),
-        w_here,
-        preferred_element_type=jnp.float32,
-    ).astype(jnp.bfloat16)
+    local = jnp.dot(hidden, w_qkv, preferred_element_type=jnp.float32).astype(jnp.bfloat16)
+    local = local.reshape(local.shape[0], heads_n, columns)
+    grouped = lax.all_to_all(local, "head", split_axis=1, concat_axis=0, tiled=True)
+    grouped = grouped.reshape(grouped.shape[0], columns)
     group_rows = grouped.shape[0]
     shaped = grouped.reshape(group_rows, groups_here, QPK + 2, HD)
     queries = shaped[:, :, :QPK]
@@ -81,16 +79,13 @@
     attended = attended.reshape(group_rows, groups_here * QPK * HD).astype(jnp.bfloat16)
     own_tokens = lax.all_to_all(attended, "head", split_axis=0, concat_axis=1, tiled=True)
     mixed = jnp.dot(own_tokens, w_out, preferred_element_type=jnp.float32).astype(jnp.bfloat16)
-    page_count = group_rows // PAGE
-    pages = keyvals.reshape(page_count, PAGE, groups_here, 2 * HD)
-    table_mine = lax.dynamic_slice_in_dim(page_table, seq_at * page_count, page_count, 0)
-    order = jnp.argsort(table_mine // page_count, stable=True)
-    received = lax.all_to_all(pages[order], "seq", split_axis=0, concat_axis=0, tiled=True)
-    arriving = jnp.argsort((page_table // page_count != seq_at).astype(jnp.int32), stable=True)[
-        :page_count
-    ]
-    slots = page_table[arriving] % page_count
-    kv_pool = jnp.zeros_like(received).at[slots].set(received).transpose(2, 0, 1, 3)
+    pages_n = page_table.shape[0]
+    page_count = pages_n // lax.axis_size("seq")
+    all_pages = piece.reshape(pages_n, PAGE, groups_here, 2 * HD)
+    wanted = seq_at * page_count + jnp.arange(page_count, dtype=jnp.int32)
+    hits = page_table[None, :] == wanted[:, None]
+    logical = jnp.sum(jnp.where(hits, jnp.arange(pages_n, dtype=jnp.int32)[None, :], 0), axis=1)
+    kv_pool = jnp.take(all_pages, logical, axis=0).transpose(2, 0, 1, 3)
     return (mixed, kv_pool)
 
 

time: 194 us -> 196 us (1.010); the launches traced: 190 us -> 197 us
  waiting for transfers between devices: 71.9 us -> 32.4 us
  blocking collectives: 0 us -> 24.8 us
  local copies, waits for them, and re-layouts: 18.6 us -> 39.9 us
  matrix products: 38.4 us -> 47.6 us
  other arithmetic: 23.1 us -> 17.7 us
  starting transfers between devices: 8.87 us -> 4.64 us
    all_gather x1 -> x0, waiting for transfers between devices: 48.5 us -> none  [shards(): lax.all_gather(hidden, 'head', axis=0, tiled=True)]
    all_to_all x0 -> x1, blocking collectives: none -> 24.8 us  [shards(): lax.all_to_all(local, 'head', split_axis=1, concat_axis=0, tiled=True)]
    cond x3 -> x9, local copies, waits for them, and re-layouts: 0.01 us -> 17.1 us
    dot_general x3, matrix products: 17.2 us -> 24.5 us  [compute(): jnp.einsum('gcqk,kgd->gcqd', weights.astype(jnp.bfloat16), kv_block[:, :,...]
    all_gather x1, waiting for transfers between devices: 18.7 us -> 25.4 us  [shards(): piece = lax.all_gather(keyvals, 'seq', axis=0, tiled=True)]
    sort x2 -> x0, other arithmetic: 4.78 us -> none  [the longest x1 3.17 us: shards(): jnp.argsort((page_table // page_count != seq_at).astype(jnp.int32), stabl...]
    all_to_all x1 -> x0, starting transfers between devices: 4.2 us -> none  [shards(): lax.all_to_all(pages[order], 'seq', split_axis=0, concat_axis=0, tiled=True)]
    all_gather x0 -> x1, local copies, waits for them, and re-layouts: none -> 3.14 us  [shards(): piece = lax.all_gather(keyvals, 'seq', axis=0, tiled=True)]
  transfers between devices with their start and end apart: 4 -> 2, of which waited for: 3 -> 2; matrix products, arithmetic and copies ran while one was open for 36% -> 5% of each run, Pallas kernels for 0% -> 0%
where the time goes in v1:
time: 196 us; the launch traced here: 197 us
  matrix products  47.6 us (24%)
  local copies, waits for them, and re-layouts  39.9 us (20%)
  waiting for transfers between devices  32.4 us (17%)
  blocking collectives  24.8 us (13%)
  other arithmetic  17.7 us (9%)
  loops' own time  16.1 us (8%)
  between operations  14.2 us (7%)
  starting transfers between devices  4.64 us (2%)
    all_gather x1, waiting for transfers between devices, shards(): piece = lax.all_gather(keyvals, 'seq', axis=0, tiled=True)  25.4 us
    all_to_all x1, blocking collectives, shards(): lax.all_to_all(local, 'head', split_axis=1, concat_axis=0, tiled=True)  24.8 us
    dot_general x3, matrix products, compute(): jnp.einsum('gcqk,kgd->gcqd', weights.astype(jnp.bfloat16), kv_block[:, :,...  24.5 us
    cond x9, local copies, waits for them, and re-layouts  17.1 us
    another operation x1, loops' own time, shards(): lax.scan(advance, carry, jnp.arange(rows // block, dtype=jnp.int32))  15.8 us
    reduce_sum x3, other arithmetic, compute(): new_total = run_total * factor + jnp.sum(weights, axis=-1)  12 us
    dot_general x3, matrix products, compute(): jnp.einsum('qgcd,kgd->gcqk', queries, kv_block[:, :, :HD], preferred_elem...  11.3 us
    all_to_all x1, waiting for transfers between devices, shards(): lax.all_to_all(attended, 'head', split_axis=0, concat_axis=1, tiled=True)  6.99 us
  transfers between devices with their start and end apart: 2, of which 2 were waited for; matrix products, arithmetic and copies ran while one was open for 5% of the time, Pallas kernels for 0%

profile of v1, /device:TPU:6, one launch (start us, length us, event | category | flops | bytes accessed | tf_op | source)
XLA Modules:
  0.0 197.2 jit_solution(4697076027734145646)
XLA Ops:
  8.2 6.4 %convolution_convert_fusion = bf16[128,3072]{1,0:T(8,128)(2,1)S(1)} fusion(bf16[128,2048]{1,0:T(8,128)(2,1)S(1)} %copy-done, bf16[2048,3072]{1,0:T(8,128)(2,1)} %param.11), kind=kOutput, calls=%fused_computation.22 | convolution fusion | flops 1611005952 | bytes 13893632 | tf_op jit(solution)/shard_map/dot_general | solution.py:21
  14.7 24.8 %all_to_all.31 = bf16[128,4,768]{2,0,1:T(8,128)(2,1)S(1)} all-to-all(bf16[128,4,768]{2,0,1:T(8,128)(2,1)S(1)} %bitcast.78), channel_id=1, replica_groups=mesh['seq'=8,'head'=4] {'head'}, dimensions={1} | all-to-all | bytes 1572864 | tf_op jit(solution)/shard_map/all_to_all | solution.py:23
  42.1 25.4 %all-gather.2.cloned.1.call-done = bf16[4096,2,128]{0,2,1:T(8,128)(2,1)} async-done(((bf16[512,2,128]{0,2,1:T(8,128)(2,1)}), bf16[4096,2,128]{0,2,1:T(8,128)(2,1)}) %all-gather.2.cloned.1.call-update) | async-done | bytes 2097168 | tf_op jit(solution)/shard_map/all_gather | solution.py:36
  67.6 96.7 %while.14 = (s32[]{:T(128)}, f32[2,4,512]{2,1,0:T(4,128)S(1)}, f32[2,4,512]{2,1,0:T(4,128)S(1)}, f32[2,4,512,64]{2,3,1,0:T(8,128)S(1)}, s32[4]{0:T(128)S(1)}, /*...) while((s32[]{:T(128)}, f32[2,4,512]{2,1,0:T(4,128)S(1)}, ...), condition=%wide.region_5.6_spmd, body=%wide.region_0.5_spmd.sunk | while | flops 1131948032 | bytes 122985960 | solution.py:76
  80.7 23.5 %conditional.2 = ((f32[2,4,512]{2,1,0:T(4,128)S(1)}, f32[2,4,512]{2,1,0:T(4,128)S(1)}, f32[2,4,512,64]{2,3,1,0:T(8,128)S(1)})) conditional(s32[]{:T(128)} %convert_element_type.39, (f32[2,4,512]{2,1,0:T(4,128)S(1)}, f32[2,4,512]{2,1,0:T(4,128)S(1)}, f32[2,4,512,64]{2,3,1,0:T(8,128)S(1)}) %tuple.49, (s32[1024]{0:T(1024)S(1)}, s32[512]{0:T(512)S(1)}, ...), branch_computations={%region_1.1_spmd, %region_2.4_spmd} | conditional | flops 1131948032 | bytes 122973264 | solution.py:74
  82.5 3.8 %fusion = (f32[2,4,512]{2,1,0:T(4,128)S(1)}, f32[2,1024,512,4]{2,1,3,0:T(8,128)S(1)}) fusion(pred[512,1024]{0,1:T(8,128)(4,1)S(1)} %or_and_fusion, bf16[512,2,4,64]{0,3,2,1:T(8,128)(2,1)S(1)} %get-tuple-element.140, bf16[4096,2,128]{0,2,1:T(8,128)(2,1)} %get-tuple-element.139, s32[]{:T(128)} %get-tuple-element.138), kind=kOutput, calls=%fused_computation.3 | convolution fusion | flops 549449728 | bytes 18104832 | tf_op jit(solution)/shard_map/while/body/eval_jaxpr/cond/branch_1_fun/qgcd,kgd->gcqk/dot_general | solution.py:53
  86.3 5.7 %copy-done.1 = f32[2,1024,512,4]{2,1,3,0:T(8,128)} copy-done((f32[2,1024,512,4]{2,1,3,0:T(8,128)}, f32[2,1024,512,4]{2,1,3,0:T(8,128)S(1)}, u32[]{:S(2)}) %copy-start.1) | copy-done | bytes 16777240 | tf_op jit(solution)/shard_map/while/body/eval_jaxpr/cond
  92.0 4.0 %fusion.2 = f32[2,4,512]{2,1,0:T(4,128)S(1)} fusion(f32[2,1024,512,4]{2,1,3,0:T(8,128)S(1)} %get-tuple-element.208, f32[2,4,512]{2,1,0:T(4,128)S(1)} %max.4, pred[512,1024]{0,1:T(8,128)(4,1)S(1)} %or_and_fusion), kind=kLoop, calls=%fused_computation.5 | loop fusion | flops 20967424 | bytes 17334272 | tf_op jit(solution)/shard_map/while/body/eval_jaxpr/cond/branch_1_fun/reduce_sum | solution.py:65
  96.0 8.2 %fusion.6 = f32[2,4,512,64]{2,3,1,0:T(8,128)S(1)} fusion(f32[2,1024,512,4]{2,1,3,0:T(8,128)} %copy-done.1, f32[2,4,512]{2,1,0:T(4,128)S(1)} %max.4, pred[512,1024]{0,1:T(8,128)(4,1)S(1)} %or_and_fusion, f32[2,4,512,64]{2,3,1,0:T(8,128)S(1)} %get-tuple-element.142, f32[2,4,512]{2,1,0:T(4,128)S(1)} %bitcast.85, bf16[4096,2,128]{0,2,1:T(8,128)(2,1)} %get-tuple-element.139, ...), kind=kOutput, calls=%fused_computation.9 | convolution fusion | flops 558366720 | bytes 19694084 | tf_op jit(solution)/shard_map/while/body/eval_jaxpr/cond/branch_1_fun/gcqk,kgd->gcqd/dot_general | solution.py:66
  110.8 23.5 %conditional.2 = ((f32[2,4,512]{2,1,0:T(4,128)S(1)}, f32[2,4,512]{2,1,0:T(4,128)S(1)}, f32[2,4,512,64]{2,3,1,0:T(8,128)S(1)})) conditional(s32[]{:T(128)} %convert_element_type.39, (f32[2,4,512]{2,1,0:T(4,128)S(1)}, f32[2,4,512]{2,1,0:T(4,128)S(1)}, f32[2,4,512,64]{2,3,1,0:T(8,128)S(1)}) %tuple.49, (s32[1024]{0:T(1024)S(1)}, s32[512]{0:T(512)S(1)}, ...), branch_computations={%region_1.1_spmd, %region_2.4_spmd} | conditional | flops 1131948032 | bytes 122973264 | solution.py:74
  112.5 3.8 %fusion = (f32[2,4,512]{2,1,0:T(4,128)S(1)}, f32[2,1024,512,4]{2,1,3,0:T(8,128)S(1)}) fusion(pred[512,1024]{0,1:T(8,128)(4,1)S(1)} %or_and_fusion, bf16[512,2,4,64]{0,3,2,1:T(8,128)(2,1)S(1)} %get-tuple-element.140, bf16[4096,2,128]{0,2,1:T(8,128)(2,1)} %get-tuple-element.139, s32[]{:T(128)} %get-tuple-element.138), kind=kOutput, calls=%fused_computation.3 | convolution fusion | flops 549449728 | bytes 18104832 | tf_op jit(solution)/shard_map/while/body/eval_jaxpr/cond/branch_1_fun/qgcd,kgd->gcqk/dot_general | solution.py:53
  116.3 5.7 %copy-done.1 = f32[2,1024,512,4]{2,1,3,0:T(8,128)} copy-done((f32[2,1024,512,4]{2,1,3,0:T(8,128)}, f32[2,1024,512,4]{2,1,3,0:T(8,128)S(1)}, u32[]{:S(2)}) %copy-start.1) | copy-done | bytes 16777240 | tf_op jit(solution)/shard_map/while/body/eval_jaxpr/cond
  122.0 4.0 %fusion.2 = f32[2,4,512]{2,1,0:T(4,128)S(1)} fusion(f32[2,1024,512,4]{2,1,3,0:T(8,128)S(1)} %get-tuple-element.208, f32[2,4,512]{2,1,0:T(4,128)S(1)} %max.4, pred[512,1024]{0,1:T(8,128)(4,1)S(1)} %or_and_fusion), kind=kLoop, calls=%fused_computation.5 | loop fusion | flops 20967424 | bytes 17334272 | tf_op jit(solution)/shard_map/while/body/eval_jaxpr/cond/branch_1_fun/reduce_sum | solution.py:65
  126.1 8.2 %fusion.6 = f32[2,4,512,64]{2,3,1,0:T(8,128)S(1)} fusion(f32[2,1024,512,4]{2,1,3,0:T(8,128)} %copy-done.1, f32[2,4,512]{2,1,0:T(4,128)S(1)} %max.4, pred[512,1024]{0,1:T(8,128)(4,1)S(1)} %or_and_fusion, f32[2,4,512,64]{2,3,1,0:T(8,128)S(1)} %get-tuple-element.142, f32[2,4,512]{2,1,0:T(4,128)S(1)} %bitcast.85, bf16[4096,2,128]{0,2,1:T(8,128)(2,1)} %get-tuple-element.139, ...), kind=kOutput, calls=%fused_computation.9 | convolution fusion | flops 558366720 | bytes 19694084 | tf_op jit(solution)/shard_map/while/body/eval_jaxpr/cond/branch_1_fun/gcqk,kgd->gcqd/dot_general | solution.py:66
  140.8 23.4 %conditional.2 = ((f32[2,4,512]{2,1,0:T(4,128)S(1)}, f32[2,4,512]{2,1,0:T(4,128)S(1)}, f32[2,4,512,64]{2,3,1,0:T(8,128)S(1)})) conditional(s32[]{:T(128)} %convert_element_type.39, (f32[2,4,512]{2,1,0:T(4,128)S(1)}, f32[2,4,512]{2,1,0:T(4,128)S(1)}, f32[2,4,512,64]{2,3,1,0:T(8,128)S(1)}) %tuple.49, (s32[1024]{0:T(1024)S(1)}, s32[512]{0:T(512)S(1)}, ...), branch_computations={%region_1.1_spmd, %region_2.4_spmd} | conditional | flops 1131948032 | bytes 122973264 | solution.py:74
  142.5 3.7 %fusion = (f32[2,4,512]{2,1,0:T(4,128)S(1)}, f32[2,1024,512,4]{2,1,3,0:T(8,128)S(1)}) fusion(pred[512,1024]{0,1:T(8,128)(4,1)S(1)} %or_and_fusion, bf16[512,2,4,64]{0,3,2,1:T(8,128)(2,1)S(1)} %get-tuple-element.140, bf16[4096,2,128]{0,2,1:T(8,128)(2,1)} %get-tuple-element.139, s32[]{:T(128)} %get-tuple-element.138), kind=kOutput, calls=%fused_computation.3 | convolution fusion | flops 549449728 | bytes 18104832 | tf_op jit(solution)/shard_map/while/body/eval_jaxpr/cond/branch_1_fun/qgcd,kgd->gcqk/dot_general | solution.py:53
  146.3 5.7 %copy-done.1 = f32[2,1024,512,4]{2,1,3,0:T(8,128)} copy-done((f32[2,1024,512,4]{2,1,3,0:T(8,128)}, f32[2,1024,512,4]{2,1,3,0:T(8,128)S(1)}, u32[]{:S(2)}) %copy-start.1) | copy-done | bytes 16777240 | tf_op jit(solution)/shard_map/while/body/eval_jaxpr/cond
  152.0 4.0 %fusion.2 = f32[2,4,512]{2,1,0:T(4,128)S(1)} fusion(f32[2,1024,512,4]{2,1,3,0:T(8,128)S(1)} %get-tuple-element.208, f32[2,4,512]{2,1,0:T(4,128)S(1)} %max.4, pred[512,1024]{0,1:T(8,128)(4,1)S(1)} %or_and_fusion), kind=kLoop, calls=%fused_computation.5 | loop fusion | flops 20967424 | bytes 17334272 | tf_op jit(solution)/shard_map/while/body/eval_jaxpr/cond/branch_1_fun/reduce_sum | solution.py:65
  156.1 8.2 %fusion.6 = f32[2,4,512,64]{2,3,1,0:T(8,128)S(1)} fusion(f32[2,1024,512,4]{2,1,3,0:T(8,128)} %copy-done.1, f32[2,4,512]{2,1,0:T(4,128)S(1)} %max.4, pred[512,1024]{0,1:T(8,128)(4,1)S(1)} %or_and_fusion, f32[2,4,512,64]{2,3,1,0:T(8,128)S(1)} %get-tuple-element.142, f32[2,4,512]{2,1,0:T(4,128)S(1)} %bitcast.85, bf16[4096,2,128]{0,2,1:T(8,128)(2,1)} %get-tuple-element.139, ...), kind=kOutput, calls=%fused_computation.9 | convolution fusion | flops 558366720 | bytes 19694084 | tf_op jit(solution)/shard_map/while/body/eval_jaxpr/cond/branch_1_fun/gcqk,kgd->gcqd/dot_general | solution.py:66
  165.4 4.6 %all-to-all-start.1 = ((bf16[4,128,512]{1,2,0:T(8,128)(2,1)}), bf16[4,128,512]{1,2,0:T(8,128)(2,1)S(1)}, u32[]{:S(2)}, u32[]{:S(2)}) async-start(bf16[4,128,512]{1,2,0:T(8,128)(2,1)} %copy.32), calls=%async_computation.1 | async-start | bytes 1048576 | tf_op jit(solution)/shard_map/all_to_all | solution.py:80
  170.0 3.1 %copy.33 = bf16[4096,2,128]{2,0,1:T(8,128)(2,1)S(1)} copy(bf16[4096,2,128]{0,2,1:T(8,128)(2,1)} %get-tuple-element.352) | data formatting | bytes 4194304 | tf_op jit(solution)/shard_map/all_gather | solution.py:36
  174.9 2.2 %gather_fusion = bf16[32,16,2,128]{3,1,2,0:T(8,128)(2,1)S(1)} fusion(bf16[256,16,2,128]{3,1,2,0:T(8,128)(2,1)} %copy.34, s32[1024]{0:T(1024)S(1)} %pad_clamp_fusion), kind=kCustom, calls=%fused_computation | custom fusion | bytes 524416 | tf_op jit(solution)/shard_map/jit(_take)/gather | solution.py:88
  177.9 7.0 %all-to-all-done.1 = bf16[4,128,512]{1,2,0:T(8,128)(2,1)S(1)} async-done(((bf16[4,128,512]{1,2,0:T(8,128)(2,1)}), bf16[4,128,512]{1,2,0:T(8,128)(2,1)S(1)}, u32[]{:S(2)}, u32[]{:S(2)}) %all-to-all-start.1) | async-done | bytes 524320 | tf_op jit(solution)/shard_map/all_to_all | solution.py:80
  184.9 5.5 %convolution_convert_fusion.1 = bf16[128,2048]{1,0:T(8,128)(2,1)} fusion(bf16[128,2048]{0,1:T(8,128)(2,1)S(1)} %bitcast.76, bf16[2048,2048]{1,0:T(8,128)(2,1)} %param.12), kind=kOutput, calls=%fused_computation.23 | convolution fusion | flops 1074003968 | bytes 9437184 | tf_op jit(solution)/shard_map/dot_general | solution.py:81
  (70 shorter events, 23.2 us)
Async XLA Ops:
  7.2 1.0 copy-start
  7.2 34.7 %copy-start.2 = (s32[256]{0:T(256)S(1)}, s32[256]{0:T(256)}, u32[]{:S(2)}) copy-start(s32[256]{0:T(256)} %param.15) | copy-start | bytes 3076
  7.2 60.3 %all-gather.2.cloned.1.call-start = ((), (), s32[]{:S(2)}) async-start(), calls=%async_computation.2 | async-start | bytes 2359296 | tf_op jit(solution)/shard_map/all_gather | solution.py:36
  86.2 5.7 %copy-start.1 = (f32[2,1024,512,4]{2,1,3,0:T(8,128)}, f32[2,1024,512,4]{2,1,3,0:T(8,128)S(1)}, u32[]{:S(2)}) copy-start(f32[2,1024,512,4]{2,1,3,0:T(8,128)S(1)} %get-tuple-element.208) | copy-start | bytes 50331652 | tf_op jit(solution)/shard_map/while/body/eval_jaxpr/cond
  116.3 5.7 %copy-start.1 = (f32[2,1024,512,4]{2,1,3,0:T(8,128)}, f32[2,1024,512,4]{2,1,3,0:T(8,128)S(1)}, u32[]{:S(2)}) copy-start(f32[2,1024,512,4]{2,1,3,0:T(8,128)S(1)} %get-tuple-element.208) | copy-start | bytes 50331652 | tf_op jit(solution)/shard_map/while/body/eval_jaxpr/cond
  146.3 5.7 %copy-start.1 = (f32[2,1024,512,4]{2,1,3,0:T(8,128)}, f32[2,1024,512,4]{2,1,3,0:T(8,128)S(1)}, u32[]{:S(2)}) copy-start(f32[2,1024,512,4]{2,1,3,0:T(8,128)S(1)} %get-tuple-element.208) | copy-start | bytes 50331652 | tf_op jit(solution)/shard_map/while/body/eval_jaxpr/cond
  165.4 19.5 %all-to-all-start.1 = ((bf16[4,128,512]{1,2,0:T(8,128)(2,1)}), bf16[4,128,512]{1,2,0:T(8,128)(2,1)S(1)}, u32[]{:S(2)}, u32[]{:S(2)}) async-start(bf16[4,128,512]{1,2,0:T(8,128)(2,1)} %copy.32), calls=%async_computation.1 | async-start | bytes 1048576 | tf_op jit(solution)/shard_map/all_to_all | solution.py:80
Sparse Core Ops, SparseCore 0:
  41.2 26.2 all-gather.1
